TPU v7x, 256 devices: a whole 4x4x8 slice. The times are simulated.
256 devices in a mesh: target: 32 (over x_lo, z, core), surface: 8 (over x_hi, y).
Axes of the slice: x: 4 (x_hi: 2, x_lo: 2; x = x_hi * 2 + x_lo), y: 4, z: 8, core: 2. Of those that a mesh axis runs over, the one named last changes fastest.
Arguments:
- response: float32 [64, 32, 32, 512], P('target', None, 'surface'), may hold values from -6 to 6
- data_spectra: bfloat16 [32, 16, 2, 32, 32, 256], P('target', None, None, 'surface'), may hold values from -0.01171875 to 0.01171875
- observed: bfloat16 [32, 2, 32, 32, 256], P('target', None, None, 'surface'), may hold values from -6 to 6
- block_lists: int32 [32, 16], replicated, may hold values from 0 to 63, as said below
Outputs:
- response_next: float32 [64, 32, 32, 512], P('target', None, 'surface')
- response_copy: bfloat16 [64, 32, 32, 512], P('target', None, 'surface')
- residual: float32 [32, 2, 32, 32, 256], P('target', None, None, 'surface')
Inputs may be any that keep to these rules, and one draw needn't show every extreme that they name: `block_lists`: block b is owned by index b // 2 of target. Each tile lists 16 blocks, no two of the same owner.
All inputs are finite; a program needn't handle non-finite values.
Results may differ from a plain program's by a relative error of at most 0.0048.
Values may be sent and summed in bfloat16 or wider, within the bound.
No kernel may reach another device: no remote copies, remote signals or barrier semaphores. Data moves between devices by JAX's collectives and lax.ppermute only.
A program may use at most 128 MiB of HBM per device.

v0:
```python
import math
import jax
import jax.numpy as jnp
from jax import lax
from jax.sharding import PartitionSpec as P

step_length = 0.5


def make_table(samples):
    freqs = samples // 2
    sample_index = lax.broadcasted_iota(jnp.int32, (samples, freqs), 0)
    freq_index = lax.broadcasted_iota(jnp.int32, (samples, freqs), 1)
    phase = (sample_index * freq_index % samples).astype(jnp.float32) * (2.0 * math.pi / samples)
    return jnp.concatenate([jnp.cos(phase), -jnp.sin(phase)], axis=1)


def contract(spec, listed):
    return jnp.einsum("lakf,lkrf->arf", spec, listed, preferred_element_type=jnp.float32)


def correlate(misfit_part, listed):
    return jnp.einsum("arf,lkrf->lakf", misfit_part, listed, preferred_element_type=jnp.float32)


def per_device(response, data_spectra, observed, block_lists):
    owners = lax.axis_size("target")
    my_index = lax.axis_index("target")
    owned = response.shape[0]
    samples = response.shape[3]
    freqs = samples // 2
    dft_table = make_table(samples)
    table_half = dft_table.astype(jnp.bfloat16)
    own_ids = lax.dynamic_slice_in_dim(block_lists, my_index, 1, 0)[0]
    own_owner = own_ids // owned
    wanted = block_lists // owned == my_index
    present = jnp.any(wanted, axis=1)
    slot_for = jnp.sum(jnp.where(wanted, block_lists % owned, 0), axis=1)
    picker = (
        (slot_for[None, :] == jnp.arange(owned, dtype=jnp.int32)[:, None]) & present[None, :]
    ).astype(jnp.float32)
    present_rows = present[:, None, None, None]
    zero_half = jnp.zeros((), jnp.bfloat16)
    copy_now = response.astype(jnp.bfloat16)
    outgoing = jnp.where(present_rows, copy_now[slot_for], zero_half)
    arrived = lax.all_to_all(outgoing, "target", split_axis=0, concat_axis=0, tiled=True)
    spectra = jnp.dot(arrived[own_owner], table_half, preferred_element_type=jnp.float32).astype(
        jnp.bfloat16
    )
    listed_data = data_spectra[0]
    spec_real = spectra[..., :freqs]
    spec_imag = spectra[..., freqs:]
    data_real = listed_data[:, 0]
    data_imag = listed_data[:, 1]
    partial_value = jnp.stack(
        [
            contract(spec_real, data_real) - contract(spec_imag, data_imag),
            contract(spec_real, data_imag) + contract(spec_imag, data_real),
        ]
    )
    observed_share = observed[0].astype(jnp.float32)
    summed_share = lax.psum_scatter(partial_value, "surface", scatter_dimension=2, tiled=True)
    residual_share = observed_share - summed_share
    misfit = lax.all_gather(residual_share.astype(jnp.bfloat16), "surface", axis=2, tiled=True)
    misfit_real = misfit[0]
    misfit_imag = misfit[1]
    grad_spectra = jnp.concatenate(
        [
            -(correlate(misfit_real, data_real) + correlate(misfit_imag, data_imag)),
            correlate(misfit_real, data_imag) - correlate(misfit_imag, data_real),
        ],
        axis=-1,
    )
    grad_time = jnp.dot(grad_spectra, dft_table.T, precision=lax.Precision.HIGHEST)
    returning = jnp.zeros((owners,) + grad_time.shape[1:], jnp.float32).at[own_owner].set(grad_time)
    received = lax.all_to_all(returning, "target", split_axis=0, concat_axis=0, tiled=True)
    flat = received.reshape(owners, -1)
    gradient = jnp.dot(picker, flat, precision=lax.Precision.HIGHEST).reshape(response.shape)
    response_next = response - step_length * gradient
    return (response_next, response_next.astype(jnp.bfloat16), residual_share[None])


def solution(mesh):
    return jax.shard_map(
        per_device,
        mesh=mesh,
        in_specs=(
            P("target", None, "surface", None),
            P("target", None, None, "surface", None, None),
            P("target", None, None, "surface", None),
            P(),
        ),
        out_specs=(
            P("target", None, "surface", None),
            P("target", None, "surface", None),
            P("target", None, None, "surface", None),
        ),
        check_vma=False,
    )
```

profile of v0, /device:TPU:96, one launch (start us, length us, event | category | flops | bytes accessed | tf_op | source)
XLA Modules:
  0.0 651.4 jit_solution(16325674682704119219)
XLA Ops:
  21.3 8.9 %all-to-all-start = ((bf16[32,32,4,512]{3,2,1,0:T(4,128)(2,1)}), bf16[32,32,4,512]{3,2,1,0:T(4,128)(2,1)}, u32[]{:S(2)}, u32[]{:S(2)}) async-start(bf16[32,32,4,512]{3,2,1,0:T(4,128)(2,1)} %broadcast_select_fusion), calls=%async_computation | async-start | bytes 8388608 | tf_op jit(solution)/shard_map/all_to_all | solution.py:46
  30.5 12.0 %copy.72 = bf16[1,16,2,4,32,256]{4,1,3,5,2,0:T(8,128)(2,1)} copy(bf16[1,16,2,4,32,256]{5,4,3,2,1,0:T(8,128)(2,1)S(1)} %copy-done.4) | data formatting | bytes 4194304 | tf_op args[1]
  44.8 81.4 %all-to-all-done = bf16[32,32,4,512]{3,2,1,0:T(4,128)(2,1)} async-done(((bf16[32,32,4,512]{3,2,1,0:T(4,128)(2,1)}), bf16[32,32,4,512]{3,2,1,0:T(4,128)(2,1)}, u32[]{:S(2)}, u32[]{:S(2)}) %all-to-all-start) | async-done | bytes 4194336 | tf_op jit(solution)/shard_map/all_to_all | solution.py:46
  132.3 6.5 copy.73
  138.8 6.7 %copy.74 = bf16[16,32,4,256]{1,0,2,3:T(8,128)(2,1)} copy(bf16[16,32,4,256]{3,1,2,0:T(8,128)(2,1)S(1)} %get-tuple-element.21) | data formatting | bytes 2097152 | tf_op jit(solution)/shard_map/slice | solution.py:52
  145.6 6.9 %fusion.9 = f32[256,32,32,1]{2,1,3,0:T(8,128)} fusion(bf16[16,32,4,256]{1,0,2,3:T(8,128)(2,1)} %copy.74, bf16[16,2,4,32,256]{3,0,2,4,1:T(8,128)(2,1)} %bitcast.108), kind=kOutput, calls=%fused_computation.20 | convolution fusion | flops 33554432 | bytes 9437184 | tf_op jit(solution)/shard_map/lakf,lkrf->arf/dot_general | solution.py:19
  171.6 8.0 %copy.77 = f32[2,32,32,256]{3,1,0,2:T(8,128)} copy(f32[2,32,32,256]{2,1,3,0:T(8,128)} %pad_maximum_fusion) | data formatting | bytes 4194304 | tf_op jit(solution)/shard_map/stack | solution.py:55
  179.7 79.2 %reduce-scatter.2.cloned.1.call-done = f32[2,32,4,256]{3,1,0,2:T(8,128)} async-done(((f32[2,32,32,256]{3,1,0,2:T(8,128)}), f32[2,32,4,256]{3,1,0,2:T(8,128)}) %reduce-scatter.2.cloned.1.call-update) | async-done | bytes 262160 | tf_op jit(solution)/shard_map/reduce_scatter | solution.py:62
  260.5 51.9 %all-gather.2.cloned.1.call-done = bf16[2,32,32,256]{3,1,0,2:T(8,128)(2,1)} async-done(((bf16[2,32,4,256]{3,1,0,2:T(8,128)(2,1)}), bf16[2,32,32,256]{3,1,0,2:T(8,128)(2,1)}) %all-gather.2.cloned.1.call-update) | async-done | bytes 1048592 | tf_op jit(solution)/shard_map/all_gather | solution.py:64
  314.6 14.5 %copy.97 = bf16[1,32,32,256]{2,1,3,0:T(8,128)(2,1)S(1)} copy(bf16[1,32,32,256]{3,1,0,2:T(8,128)(2,1)} %get-tuple-element.23) | data formatting | bytes 1048576
  329.2 6.6 %fusion.11 = f32[256,32,16,4]{1,2,3,0:T(8,128)} fusion(bf16[16,2,4,32,256]{3,0,2,4,1:T(8,128)(2,1)} %bitcast.110, bf16[1,32,32,256]{2,1,3,0:T(8,128)(2,1)S(1)} %copy.97), kind=kOutput, calls=%fused_computation.22 | convolution fusion | flops 33554432 | bytes 6815744 | tf_op jit(solution)/shard_map/arf,lkrf->lakf/dot_general | solution.py:23
  335.8 6.7 %fusion.8 = f32[256,32,16,4]{1,2,3,0:T(8,128)} fusion(bf16[16,2,4,32,256]{3,0,2,4,1:T(8,128)(2,1)} %bitcast.111, bf16[1,32,32,256]{2,1,3,0:T(8,128)(2,1)S(1)} %copy.97), kind=kOutput, calls=%fused_computation.19 | convolution fusion | flops 33554432 | bytes 6815744 | tf_op jit(solution)/shard_map/arf,lkrf->lakf/dot_general | solution.py:23
  346.9 9.1 %subtract_bitcast_fusion = f32[16,32,4,256]{1,0,2,3:T(8,128)} fusion(f32[256,32,16,4]{1,2,3,0:T(8,128)} %fusion.11, bf16[16,2,4,32,256]{3,0,2,4,1:T(8,128)(2,1)} %bitcast.112, bf16[1,32,32,256]{2,1,3,0:T(8,128)(2,1)S(1)} %copy.98), kind=kOutput, calls=%fused_computation.6 | convolution fusion | flops 34078720 | bytes 15204352 | tf_op jit(solution)/shard_map/arf,lkrf->lakf/dot_general | solution.py:23
  356.1 7.4 %copy.81 = f32[16,32,4,256]{3,1,2,0:T(8,128)} copy(f32[16,32,4,256]{1,0,2,3:T(8,128)} %subtract_bitcast_fusion) | data formatting | bytes 4194304 | tf_op jit(solution)/shard_map/sub | solution.py:70
  363.4 9.1 %negate_bitcast_fusion = f32[16,32,4,256]{1,0,2,3:T(8,128)} fusion(f32[256,32,16,4]{1,2,3,0:T(8,128)} %fusion.8, bf16[16,2,4,32,256]{3,0,2,4,1:T(8,128)(2,1)} %bitcast.113, bf16[1,32,32,256]{2,1,3,0:T(8,128)(2,1)S(1)} %copy.98), kind=kOutput, calls=%fused_computation.7 | convolution fusion | flops 34603008 | bytes 15204352 | tf_op jit(solution)/shard_map/arf,lkrf->lakf/dot_general | solution.py:23
  372.6 7.6 %copy.80 = f32[16,32,4,256]{3,1,2,0:T(8,128)} copy(f32[16,32,4,256]{1,0,2,3:T(8,128)} %negate_bitcast_fusion) | data formatting | bytes 4194304 | tf_op jit(solution)/shard_map/neg | solution.py:69
  380.2 9.6 %fusion.2 = f32[16,32,4,512]{3,1,2,0:T(8,128)} fusion(f32[16,32,4,256]{3,1,2,0:T(8,128)S(1)} %copy-done.3, f32[16,32,4,256]{3,1,2,0:T(8,128)} %copy.80, f32[512,256]{1,0:T(8,128)S(1)} %get-tuple-element.28, f32[512,256]{1,0:T(8,128)S(1)} %get-tuple-element.29), kind=kOutput, calls=%fused_computation.10 | convolution fusion | flops 6443761664 | bytes 9437184 | tf_op jit(solution)/shard_map/dot_general | solution.py:74
  394.1 8.1 %scatter_fusion = f32[32,32,4,512]{3,1,2,0:T(8,128)} fusion(f32[32,32,4,512]{3,1,2,0:T(8,128)} %broadcast_in_dim.18, s32[16]{0:T(128)S(1)} %fusion.52, f32[16,32,4,512]{3,1,2,0:T(8,128)} %fusion.2), kind=kCustom, calls=%fused_computation.2 | custom fusion | bytes 12582976 | tf_op jit(solution)/shard_map/scatter | solution.py:75
  402.2 7.8 %all-to-all-start.1 = ((f32[32,32,4,512]{3,1,2,0:T(8,128)}), f32[32,32,4,512]{3,1,2,0:T(8,128)}, u32[]{:S(2)}, u32[]{:S(2)}) async-start(f32[32,32,4,512]{3,1,2,0:T(8,128)} %scatter_fusion), calls=%async_computation.2 | async-start | bytes 16777216 | tf_op jit(solution)/shard_map/all_to_all | solution.py:76
  410.9 187.1 %all-to-all-done.1 = f32[32,32,4,512]{3,1,2,0:T(8,128)} async-done(((f32[32,32,4,512]{3,1,2,0:T(8,128)}), f32[32,32,4,512]{3,1,2,0:T(8,128)}, u32[]{:S(2)}, u32[]{:S(2)}) %all-to-all-start.1) | async-done | bytes 8388640 | tf_op jit(solution)/shard_map/all_to_all | solution.py:76
  598.0 13.8 %copy.82 = f32[32,32,4,512]{3,2,1,0:T(4,128)} copy(f32[32,32,4,512]{3,1,2,0:T(8,128)} %all-to-all-done.1) | data formatting | bytes 16777216 | tf_op jit(solution)/shard_map/all_to_all | solution.py:76
  611.8 9.8 %reshape.108 = f32[32,65536]{1,0:T(8,128)} reshape(f32[32,32,4,512]{3,2,1,0:T(4,128)} %copy.82) | data formatting | bytes 16777216 | tf_op jit(solution)/shard_map/reshape | solution.py:77
  621.6 10.0 %dot_general.48 = f32[32,4,512,32]{2,1,0,3:T(4,128)} reshape(f32[65536,32]{0,1:T(8,128)} %bitcast.118) | data formatting | bytes 16777216 | tf_op jit(solution)/shard_map/dot_general | solution.py:78
  631.6 10.8 %fusion.61 = (bf16[2,32,4,512]{3,0,2,1:T(2,128)(2,1)S(1)}, f32[2,32,4,512]{3,0,2,1:T(2,128)S(1)}) fusion(f32[32,4,512,32]{2,1,0,3:T(4,128)} %dot_general.48, pred[32]{0:T(512)(128)(4,1)S(1)} %get-tuple-element.18, s32[32]{0:T(128)S(1)} %fusion.44, f32[2,32,4,512]{3,2,1,0:T(4,128)S(1)} %copy-done.5), kind=kOutput, calls=%fused_computation.86 | convolution fusion | flops 50724992 | bytes 9699488 | tf_op jit(solution)/shard_map/dot_general | solution.py:78
  (50 shorter events, 57.2 us)
Async XLA Ops:
  21.3 9.2 %copy-start.4 = (bf16[1,16,2,4,32,256]{5,4,3,2,1,0:T(8,128)(2,1)S(1)}, bf16[1,16,2,4,32,256]{5,4,3,2,1,0:T(8,128)(2,1)}, u32[]{:S(2)}) copy-start(bf16[1,16,2,4,32,256]{5,4,3,2,1,0:T(8,128)(2,1)} %param.5) | copy-start | bytes 6291460
  21.3 104.9 %all-to-all-start = ((bf16[32,32,4,512]{3,2,1,0:T(4,128)(2,1)}), bf16[32,32,4,512]{3,2,1,0:T(4,128)(2,1)}, u32[]{:S(2)}, u32[]{:S(2)}) async-start(bf16[32,32,4,512]{3,2,1,0:T(4,128)(2,1)} %broadcast_select_fusion), calls=%async_computation | async-start | bytes 8388608 | tf_op jit(solution)/shard_map/all_to_all | solution.py:46
  30.2 228.6 %reduce-scatter.2.cloned.1.call-start = ((), (), s32[]{:S(2)}) async-start(), calls=%async_computation.3 | async-start | bytes 2359296 | tf_op jit(solution)/shard_map/reduce_scatter | solution.py:62
  30.5 12.0 %copy-start.7 = (s32[32,16]{0,1:T(8,128)S(1)}, s32[32,16]{0,1:T(8,128)}, u32[]{:S(2)}) copy-start(s32[32,16]{0,1:T(8,128)} %param.7) | copy-start | bytes 6148
  145.6 6.9 %copy-start = (bf16[16,32,4,256]{1,0,2,3:T(8,128)(2,1)S(1)}, bf16[16,32,4,256]{1,0,2,3:T(8,128)(2,1)}, u32[]{:S(2)}) copy-start(bf16[16,32,4,256]{1,0,2,3:T(8,128)(2,1)} %copy.73) | copy-start | bytes 3145732
  145.6 10.6 %slice-start = ((s8[8388608]{0:T(1024)(128)(4,1)}), s8[4194304]{0:T(1024)(128)(4,1)S(1)}, s32[]{:S(2)}) async-start(s8[8388608]{0:T(1024)(128)(4,1)} %bitcast.114), calls=%async_computation.5 | async-start | bytes 8388608
  152.5 3.7 slice-start.1
  156.2 5.7 copy-start.1
  161.9 3.2 copy-start.2
  171.6 87.2 %copy-start.6 = (bf16[1,2,32,4,256]{4,3,2,1,0:T(4,128)(2,1)S(1)}, bf16[1,2,32,4,256]{4,3,2,1,0:T(4,128)(2,1)}, u32[]{:S(2)}) copy-start(bf16[1,2,32,4,256]{4,3,2,1,0:T(4,128)(2,1)} %param.6) | copy-start | bytes 393220
  179.6 132.8 %all-gather.2.cloned.1.call-start = ((), (), s32[]{:S(2)}) async-start(), calls=%async_computation.4 | async-start | bytes 1179648 | tf_op jit(solution)/shard_map/all_gather | solution.py:64
  372.6 7.6 %copy-start.3 = (f32[16,32,4,256]{3,1,2,0:T(8,128)S(1)}, f32[16,32,4,256]{3,1,2,0:T(8,128)}, u32[]{:S(2)}) copy-start(f32[16,32,4,256]{3,1,2,0:T(8,128)} %copy.81) | copy-start | bytes 6291460
  402.2 195.8 %all-to-all-start.1 = ((f32[32,32,4,512]{3,1,2,0:T(8,128)}), f32[32,32,4,512]{3,1,2,0:T(8,128)}, u32[]{:S(2)}, u32[]{:S(2)}) async-start(f32[32,32,4,512]{3,1,2,0:T(8,128)} %scatter_fusion), calls=%async_computation.2 | async-start | bytes 16777216 | tf_op jit(solution)/shard_map/all_to_all | solution.py:76
  621.6 10.0 %copy-start.5 = (f32[2,32,4,512]{3,2,1,0:T(4,128)S(1)}, f32[2,32,4,512]{3,2,1,0:T(4,128)}, u32[]{:S(2)}) copy-start(f32[2,32,4,512]{3,2,1,0:T(4,128)} %param.4) | copy-start | bytes 1572868
Sparse Core Ops, SparseCore 0:
  179.7 79.0 reduce-scatter.1
  262.1 50.2 all-gather.1
where the time goes:
time: 656 us; the launch traced here: 651 us
  waiting for transfers between devices  400 us (61%)
  local copies, waits for them, and re-layouts  129 us (20%)
  matrix products  72.7 us (11%)
  other arithmetic  18.7 us (3%)
  starting transfers between devices  17 us (3%)
  between operations  14.7 us (2%)
    all_to_all x1, waiting for transfers between devices, per_device(): lax.all_to_all(returning, 'target', split_axis=0, concat_axis=0, tiled=True)  187 us
    all_to_all x1, waiting for transfers between devices, per_device(): lax.all_to_all(outgoing, 'target', split_axis=0, concat_axis=0, tiled=True)  81.4 us
    reduce_scatter x1, waiting for transfers between devices, per_device(): lax.psum_scatter(partial_value, 'surface', scatter_dimension=2, tiled=True)  79.2 us
    all_gather x1, waiting for transfers between devices, per_device(): lax.all_gather(residual_share.astype(jnp.bfloat16), 'surface', axis=2, ti...  51.9 us
    unnamed x26, local copies, waits for them, and re-layouts  33.6 us
    dot_general x4, matrix products, correlate(): jnp.einsum('arf,lkrf->lakf', misfit_part, listed, preferred_element_type=...  31.6 us
    dot_general x4, matrix products, contract(): jnp.einsum('lakf,lkrf->arf', spec, listed, preferred_element_type=jnp.flo...  19.5 us
    all_to_all x1, local copies, waits for them, and re-layouts, per_device(): lax.all_to_all(returning, 'target', split_axis=0, concat_axis=0, tiled=True)  13.8 us
  transfers between devices with their start and end apart: 4, of which 4 were waited for; matrix products, arithmetic and copies ran while one was open for 2% of the time, Pallas kernels for 0%

commit v1 on v0

--- a/solution.py
+++ b/solution.py
@@ -61,7 +61,15 @@
     observed_share = observed[0].astype(jnp.float32)
     summed_share = lax.psum_scatter(partial_value, "surface", scatter_dimension=2, tiled=True)
     residual_share = observed_share - summed_share
-    misfit = lax.all_gather(residual_share.astype(jnp.bfloat16), "surface", axis=2, tiled=True)
+    misfit = jnp.concatenate(
+        lax.all_to_all(
+            jnp.stack([residual_share.astype(jnp.bfloat16)] * lax.axis_size("surface")),
+            "surface",
+            0,
+            0,
+        ),
+        axis=2,
+    )
     misfit_real = misfit[0]
     misfit_imag = misfit[1]
     grad_spectra = jnp.concatenate(

time: 656 us -> 622 us (0.948)
  waiting for transfers between devices: 400 us -> 348 us
  blocking collectives: 0 us -> 29.8 us
  local copies, waits for them, and re-layouts: 129 us -> 117 us
    all_gather x1 -> x0, waiting for transfers between devices: 51.9 us -> none  [per_device(): lax.all_gather(residual_share.astype(jnp.bfloat16), 'surface', axis=2, ti...]
    all_to_all x0 -> x1, blocking collectives: none -> 29.8 us  [per_device(): lax.all_to_all(jnp.stack([residual_share.astype(jnp.bfloat16)] * lax.axis...]
    unnamed x26 -> x24, local copies, waits for them, and re-layouts: 33.6 us -> 14.6 us
    squeeze x0 -> x2, local copies, waits for them, and re-layouts: none -> 8.91 us  [the longest x1 4.45 us: per_device(): misfit_real = misfit[0]]
  transfers between devices with their start and end apart: 4 -> 3, of which waited for: 4 -> 3; matrix products, arithmetic and copies ran while one was open for 2% -> 2% of each run, Pallas kernels for 0% -> 0%
where the time goes in v1:
time: 622 us; the launch traced here: 618 us
  waiting for transfers between devices  348 us (56%)
  local copies, waits for them, and re-layouts  117 us (19%)
  matrix products  72.7 us (12%)
  blocking collectives  29.8 us (5%)
  other arithmetic  18 us (3%)
  starting transfers between devices  17.2 us (3%)
  between operations  14.7 us (2%)
    all_to_all x1, waiting for transfers between devices, per_device(): lax.all_to_all(returning, 'target', split_axis=0, concat_axis=0, tiled=True)  187 us
    all_to_all x1, waiting for transfers between devices, per_device(): lax.all_to_all(outgoing, 'target', split_axis=0, concat_axis=0, tiled=True)  81.4 us
    reduce_scatter x1, waiting for transfers between devices, per_device(): lax.psum_scatter(partial_value, 'surface', scatter_dimension=2, tiled=True)  79.2 us
    dot_general x4, matrix products, correlate(): jnp.einsum('arf,lkrf->lakf', misfit_part, listed, preferred_element_type=...  31.5 us
    all_to_all x1, blocking collectives, per_device(): lax.all_to_all(jnp.stack([residual_share.astype(jnp.bfloat16)] * lax.axis...  29.8 us
    dot_general x4, matrix products, contract(): jnp.einsum('lakf,lkrf->arf', spec, listed, preferred_element_type=jnp.flo...  19.5 us
    unnamed x24, local copies, waits for them, and re-layouts  14.6 us
    all_to_all x1, local copies, waits for them, and re-layouts, per_device(): lax.all_to_all(returning, 'target', split_axis=0, concat_axis=0, tiled=True)  13.8 us
  transfers between devices with their start and end apart: 3, of which 3 were waited for; matrix products, arithmetic and copies ran while one was open for 2% of the time, Pallas kernels for 0%

profile of v1, /device:TPU:96, one launch (start us, length us, event | category | flops | bytes accessed | tf_op | source)
XLA Modules:
  0.0 617.5 jit_solution(1214215365610578129)
XLA Ops:
  21.3 8.9 %all-to-all-start = ((bf16[32,32,4,512]{3,2,1,0:T(4,128)(2,1)}), bf16[32,32,4,512]{3,2,1,0:T(4,128)(2,1)}, u32[]{:S(2)}, u32[]{:S(2)}) async-start(bf16[32,32,4,512]{3,2,1,0:T(4,128)(2,1)} %broadcast_select_fusion), calls=%async_computation | async-start | bytes 8388608 | tf_op jit(solution)/shard_map/all_to_all | solution.py:46
  30.5 12.0 %copy.82 = bf16[1,16,2,4,32,256]{4,1,3,5,2,0:T(8,128)(2,1)} copy(bf16[1,16,2,4,32,256]{5,4,3,2,1,0:T(8,128)(2,1)S(1)} %copy-done.4) | data formatting | bytes 4194304 | tf_op args[1]
  44.8 81.4 %all-to-all-done = bf16[32,32,4,512]{3,2,1,0:T(4,128)(2,1)} async-done(((bf16[32,32,4,512]{3,2,1,0:T(4,128)(2,1)}), bf16[32,32,4,512]{3,2,1,0:T(4,128)(2,1)}, u32[]{:S(2)}, u32[]{:S(2)}) %all-to-all-start) | async-done | bytes 4194336 | tf_op jit(solution)/shard_map/all_to_all | solution.py:46
  132.3 6.5 %copy.83 = bf16[16,32,4,256]{1,0,2,3:T(8,128)(2,1)} copy(bf16[16,32,4,256]{3,1,2,0:T(8,128)(2,1)S(1)} %get-tuple-element.20) | data formatting | bytes 2097152 | tf_op jit(solution)/shard_map/slice | solution.py:51
  138.8 6.7 %copy.84 = bf16[16,32,4,256]{1,0,2,3:T(8,128)(2,1)} copy(bf16[16,32,4,256]{3,1,2,0:T(8,128)(2,1)S(1)} %get-tuple-element.21) | data formatting | bytes 2097152 | tf_op jit(solution)/shard_map/slice | solution.py:52
  145.6 6.9 %fusion.9 = f32[256,32,32,1]{2,1,3,0:T(8,128)} fusion(bf16[16,32,4,256]{1,0,2,3:T(8,128)(2,1)} %copy.84, bf16[16,2,4,32,256]{3,0,2,4,1:T(8,128)(2,1)} %bitcast.107), kind=kOutput, calls=%fused_computation.20 | convolution fusion | flops 33554432 | bytes 9437184 | tf_op jit(solution)/shard_map/lakf,lkrf->arf/dot_general | solution.py:19
  165.1 6.5 %pad_maximum_fusion = f32[2,32,32,256]{2,1,3,0:T(8,128)} fusion(f32[1,32,32,256]{2,1,3,0:T(8,128)S(1)} %copy-done.2, f32[1,32,32,256]{2,1,3,0:T(8,128)} %fusion.7), kind=kLoop, calls=%fused_computation.3 | loop fusion | flops 524288 | bytes 4194304 | tf_op jit(solution)/shard_map/stack | solution.py:55
  171.6 7.9 %copy.87 = f32[2,32,32,256]{3,1,0,2:T(8,128)} copy(f32[2,32,32,256]{2,1,3,0:T(8,128)} %pad_maximum_fusion) | data formatting | bytes 4194304 | tf_op jit(solution)/shard_map/stack | solution.py:55
  179.6 79.2 %reduce-scatter.2.cloned.1.call-done = f32[2,32,4,256]{3,1,0,2:T(8,128)} async-done(((f32[2,32,32,256]{3,1,0,2:T(8,128)}), f32[2,32,4,256]{3,1,0,2:T(8,128)}) %reduce-scatter.2.cloned.1.call-update) | async-done | bytes 262160 | tf_op jit(solution)/shard_map/reduce_scatter | solution.py:62
  259.9 29.8 %all_to_all.15 = bf16[8,2,32,4,256]{4,2,3,1,0:T(8,128)(2,1)S(1)} all-to-all(bf16[8,2,32,4,256]{4,2,3,1,0:T(8,128)(2,1)S(1)} %stack.11), channel_id=1, replica_groups=mesh['target'=32,'surface'=8] {'surface'}, dimensions={0} | all-to-all | bytes 2097152 | tf_op jit(solution)/shard_map/all_to_all | solution.py:65
  295.4 6.6 %fusion.11 = f32[256,32,16,4]{1,2,3,0:T(8,128)} fusion(bf16[32,32,256,1]{1,0,3,2:T(8,128)(2,1)S(1)} %copy.107, bf16[16,2,4,32,256]{3,0,2,4,1:T(8,128)(2,1)} %bitcast.109), kind=kOutput, calls=%fused_computation.22 | convolution fusion | flops 33554432 | bytes 6815744 | tf_op jit(solution)/shard_map/arf,lkrf->lakf/dot_general | solution.py:23
  302.0 6.7 %fusion.8 = f32[256,32,16,4]{1,2,3,0:T(8,128)} fusion(bf16[32,32,256,1]{1,0,3,2:T(8,128)(2,1)S(1)} %copy.107, bf16[16,2,4,32,256]{3,0,2,4,1:T(8,128)(2,1)} %bitcast.110), kind=kOutput, calls=%fused_computation.19 | convolution fusion | flops 33554432 | bytes 6815744 | tf_op jit(solution)/shard_map/arf,lkrf->lakf/dot_general | solution.py:23
  313.1 9.1 %subtract_bitcast_fusion = f32[16,32,4,256]{1,0,2,3:T(8,128)} fusion(f32[256,32,16,4]{1,2,3,0:T(8,128)} %fusion.11, bf16[32,32,256,1]{1,0,3,2:T(8,128)(2,1)S(1)} %copy.108, bf16[16,2,4,32,256]{3,0,2,4,1:T(8,128)(2,1)} %bitcast.111), kind=kOutput, calls=%fused_computation.6 | convolution fusion | flops 34078720 | bytes 15204352 | tf_op jit(solution)/shard_map/arf,lkrf->lakf/dot_general | solution.py:23
  322.2 7.4 %copy.95 = f32[16,32,4,256]{3,1,2,0:T(8,128)} copy(f32[16,32,4,256]{1,0,2,3:T(8,128)} %subtract_bitcast_fusion) | data formatting | bytes 4194304 | tf_op jit(solution)/shard_map/sub | solution.py:78
  329.6 9.1 %negate_bitcast_fusion = f32[16,32,4,256]{1,0,2,3:T(8,128)} fusion(f32[256,32,16,4]{1,2,3,0:T(8,128)} %fusion.8, bf16[32,32,256,1]{1,0,3,2:T(8,128)(2,1)S(1)} %copy.108, bf16[16,2,4,32,256]{3,0,2,4,1:T(8,128)(2,1)} %bitcast.112), kind=kOutput, calls=%fused_computation.7 | convolution fusion | flops 34603008 | bytes 15204352 | tf_op jit(solution)/shard_map/arf,lkrf->lakf/dot_general | solution.py:23
  338.7 7.5 %copy.94 = f32[16,32,4,256]{3,1,2,0:T(8,128)} copy(f32[16,32,4,256]{1,0,2,3:T(8,128)} %negate_bitcast_fusion) | data formatting | bytes 4194304 | tf_op jit(solution)/shard_map/neg | solution.py:77
  346.3 9.6 %fusion.2 = f32[16,32,4,512]{3,1,2,0:T(8,128)} fusion(f32[16,32,4,256]{3,1,2,0:T(8,128)S(1)} %copy-done.3, f32[16,32,4,256]{3,1,2,0:T(8,128)} %copy.94, f32[512,256]{1,0:T(8,128)S(1)} %get-tuple-element.28, f32[512,256]{1,0:T(8,128)S(1)} %get-tuple-element.29), kind=kOutput, calls=%fused_computation.10 | convolution fusion | flops 6443761664 | bytes 9437184 | tf_op jit(solution)/shard_map/dot_general | solution.py:82
  360.2 8.0 %scatter_fusion = f32[32,32,4,512]{3,1,2,0:T(8,128)} fusion(f32[32,32,4,512]{3,1,2,0:T(8,128)} %broadcast_in_dim.18, s32[16]{0:T(128)S(1)} %fusion.48, f32[16,32,4,512]{3,1,2,0:T(8,128)} %fusion.2), kind=kCustom, calls=%fused_computation.2 | custom fusion | bytes 12582976 | tf_op jit(solution)/shard_map/scatter | solution.py:83
  368.1 8.0 %all-to-all-start.2 = ((f32[32,32,4,512]{3,1,2,0:T(8,128)}), f32[32,32,4,512]{3,1,2,0:T(8,128)}, u32[]{:S(2)}, u32[]{:S(2)}) async-start(f32[32,32,4,512]{3,1,2,0:T(8,128)} %scatter_fusion), calls=%async_computation.3 | async-start | bytes 16777216 | tf_op jit(solution)/shard_map/all_to_all | solution.py:84
  377.0 187.1 %all-to-all-done.2 = f32[32,32,4,512]{3,1,2,0:T(8,128)} async-done(((f32[32,32,4,512]{3,1,2,0:T(8,128)}), f32[32,32,4,512]{3,1,2,0:T(8,128)}, u32[]{:S(2)}, u32[]{:S(2)}) %all-to-all-start.2) | async-done | bytes 8388640 | tf_op jit(solution)/shard_map/all_to_all | solution.py:84
  564.1 13.8 %copy.96 = f32[32,32,4,512]{3,2,1,0:T(4,128)} copy(f32[32,32,4,512]{3,1,2,0:T(8,128)} %all-to-all-done.2) | data formatting | bytes 16777216 | tf_op jit(solution)/shard_map/all_to_all | solution.py:84
  577.9 9.8 %reshape.119 = f32[32,65536]{1,0:T(8,128)} reshape(f32[32,32,4,512]{3,2,1,0:T(4,128)} %copy.96) | data formatting | bytes 16777216 | tf_op jit(solution)/shard_map/reshape | solution.py:85
  587.7 10.0 %dot_general.48 = f32[32,4,512,32]{2,1,0,3:T(4,128)} reshape(f32[65536,32]{0,1:T(8,128)} %bitcast.117) | data formatting | bytes 16777216 | tf_op jit(solution)/shard_map/dot_general | solution.py:86
  597.7 10.8 %fusion.57 = (bf16[2,32,4,512]{3,0,2,1:T(2,128)(2,1)S(1)}, f32[2,32,4,512]{3,0,2,1:T(2,128)S(1)}) fusion(f32[32,4,512,32]{2,1,0,3:T(4,128)} %dot_general.48, pred[32]{0:T(512)(128)(4,1)S(1)} %get-tuple-element.18, s32[32]{0:T(128)S(1)} %fusion.40, f32[2,32,4,512]{3,2,1,0:T(4,128)S(1)} %copy-done.5), kind=kOutput, calls=%fused_computation.83 | convolution fusion | flops 50724992 | bytes 9699488 | tf_op jit(solution)/shard_map/dot_general | solution.py:86
  (51 shorter events, 53.5 us)
Async XLA Ops:
  21.3 9.2 %copy-start.4 = (bf16[1,16,2,4,32,256]{5,4,3,2,1,0:T(8,128)(2,1)S(1)}, bf16[1,16,2,4,32,256]{5,4,3,2,1,0:T(8,128)(2,1)}, u32[]{:S(2)}) copy-start(bf16[1,16,2,4,32,256]{5,4,3,2,1,0:T(8,128)(2,1)} %param.5) | copy-start | bytes 6291460
  21.3 104.9 %all-to-all-start = ((bf16[32,32,4,512]{3,2,1,0:T(4,128)(2,1)}), bf16[32,32,4,512]{3,2,1,0:T(4,128)(2,1)}, u32[]{:S(2)}, u32[]{:S(2)}) async-start(bf16[32,32,4,512]{3,2,1,0:T(4,128)(2,1)} %broadcast_select_fusion), calls=%async_computation | async-start | bytes 8388608 | tf_op jit(solution)/shard_map/all_to_all | solution.py:46
  30.2 228.5 %reduce-scatter.2.cloned.1.call-start = ((), (), s32[]{:S(2)}) async-start(), calls=%async_computation.4 | async-start | bytes 2359296 | tf_op jit(solution)/shard_map/reduce_scatter | solution.py:62
  30.5 12.0 %copy-start.7 = (s32[32,16]{0,1:T(8,128)S(1)}, s32[32,16]{0,1:T(8,128)}, u32[]{:S(2)}) copy-start(s32[32,16]{0,1:T(8,128)} %param.7) | copy-start | bytes 6148
  145.6 6.9 %copy-start = (bf16[16,32,4,256]{1,0,2,3:T(8,128)(2,1)S(1)}, bf16[16,32,4,256]{1,0,2,3:T(8,128)(2,1)}, u32[]{:S(2)}) copy-start(bf16[16,32,4,256]{1,0,2,3:T(8,128)(2,1)} %copy.83) | copy-start | bytes 3145732
  145.6 10.6 %slice-start = ((s8[8388608]{0:T(1024)(128)(4,1)}), s8[4194304]{0:T(1024)(128)(4,1)S(1)}, s32[]{:S(2)}) async-start(s8[8388608]{0:T(1024)(128)(4,1)} %bitcast.113), calls=%async_computation.5 | async-start | bytes 8388608
  152.4 3.7 slice-start.1
  156.2 5.7 copy-start.1
  161.9 3.3 copy-start.2
  171.6 87.2 %copy-start.6 = (bf16[1,2,32,4,256]{4,3,2,1,0:T(4,128)(2,1)S(1)}, bf16[1,2,32,4,256]{4,3,2,1,0:T(4,128)(2,1)}, u32[]{:S(2)}) copy-start(bf16[1,2,32,4,256]{4,3,2,1,0:T(4,128)(2,1)} %param.6) | copy-start | bytes 393220
  338.7 7.6 %copy-start.3 = (f32[16,32,4,256]{3,1,2,0:T(8,128)S(1)}, f32[16,32,4,256]{3,1,2,0:T(8,128)}, u32[]{:S(2)}) copy-start(f32[16,32,4,256]{3,1,2,0:T(8,128)} %copy.95) | copy-start | bytes 6291460
  368.1 196.0 %all-to-all-start.2 = ((f32[32,32,4,512]{3,1,2,0:T(8,128)}), f32[32,32,4,512]{3,1,2,0:T(8,128)}, u32[]{:S(2)}, u32[]{:S(2)}) async-start(f32[32,32,4,512]{3,1,2,0:T(8,128)} %scatter_fusion), calls=%async_computation.3 | async-start | bytes 16777216 | tf_op jit(solution)/shard_map/all_to_all | solution.py:84
  587.7 10.0 %copy-start.5 = (f32[2,32,4,512]{3,2,1,0:T(4,128)S(1)}, f32[2,32,4,512]{3,2,1,0:T(4,128)}, u32[]{:S(2)}) copy-start(f32[2,32,4,512]{3,2,1,0:T(4,128)} %param.4) | copy-start | bytes 1572868
Sparse Core Ops, SparseCore 0:
  179.7 79.0 reduce-scatter.1
